TPU v7x, 512 devices: a whole 4x4x16 slice. The times are simulated.
512 devices in a mesh: frame: 32 (over x, z_lo), row: 16 (over y, z_hi, core).
Axes of the slice: x: 4, y: 4, z: 16 (z_hi: 2, z_lo: 8; z = z_hi * 8 + z_lo), core: 2. Of those that a mesh axis runs over, the one named last changes fastest.
Arguments:
- tokens: bfloat16 [32, 4096, 512], P('frame', 'row'), may hold values from -15 to 15
- norm_spatial: float32 [512], replicated, may hold values from 0.25 to 1.75
- w_spatial: bfloat16 [512, 1536], replicated, may hold values from -10 to 10
- w_spatial_out: bfloat16 [512, 512], replicated, may hold values from -0.25 to 0.25
- norm_temporal: float32 [512], replicated, may hold values from 0.25 to 1.75
- w_temporal: bfloat16 [512, 1536], replicated, may hold values from -10 to 10
- w_temporal_out: bfloat16 [512, 512], replicated, may hold values from -0.25 to 0.25
Outputs:
- mixed: bfloat16 [32, 4096, 512], P('frame', 'row')
All inputs are finite; a program needn't handle non-finite values.
Results may differ from a plain program's by a relative error of at most 0.01.
The roundings to bfloat16 on the way count: a program that leaves them out, or rounds other values in their place, can miss the bound.
Values may be sent and summed in bfloat16 or wider, within the bound.
No kernel may reach another device: no remote copies, remote signals or barrier semaphores. Data moves between devices by JAX's collectives and lax.ppermute only.
A program may use at most 64 MiB of HBM per device.

v0:
```python
import math

import jax
import jax.numpy as jnp
from jax import lax
from jax.experimental import pallas as pl
from jax.experimental.pallas import tpu as pltpu
from jax.sharding import Mesh

from jax.sharding import PartitionSpec as P

HEADS = 8
STATS = 64


def layer_norm(rows, gain):
    mean = jnp.mean(rows, axis=-1, keepdims=True)
    centred = rows - mean
    spread = jnp.mean(centred * centred, axis=-1, keepdims=True)
    return centred * lax.rsqrt(spread + 1e-05) * gain


def _scores(q_ref, k_ref, cols, scale):
    del scale
    return lax.dot_general(
        q_ref[:, cols], k_ref[:, cols], (((1,), (1,)), ((), ())),
        preferred_element_type=jnp.float32,
    )


def partial_kernel(q_ref, k_ref, v_ref, o_ref, m_ref, l_ref, *, size, scale):
    for h in range(HEADS):
        cols = slice(h * size, (h + 1) * size)
        scores = _scores(q_ref, k_ref, cols, scale)
        peak = jnp.max(scores, axis=1, keepdims=True)
        weights = jnp.exp(scores - peak)
        l_ref[:, h : h + 1] = jnp.sum(weights, axis=1, keepdims=True)
        m_ref[:, h : h + 1] = peak
        o_ref[:, cols] = jnp.dot(
            weights.astype(jnp.bfloat16), v_ref[:, cols], preferred_element_type=jnp.float32
        )


def merge_kernel(q_ref, k_ref, v_ref, o1_ref, m1_ref, l1_ref, out_ref, *, size, rows):
    width = HEADS * size
    for h in range(HEADS):
        cols = slice(h * size, (h + 1) * size)
        scores = lax.dot_general(
            q_ref[rows, cols], k_ref[:, cols], (((1,), (1,)), ((), ())),
            preferred_element_type=jnp.float32,
        )
        before = m1_ref[rows, h : h + 1]
        peak = jnp.maximum(before, jnp.max(scores, axis=1, keepdims=True))
        weights = jnp.exp(scores - peak)
        fade = jnp.exp(before - peak)
        total = l1_ref[rows, h : h + 1] * fade + jnp.sum(weights, axis=1, keepdims=True)
        out_ref[:, cols] = o1_ref[rows, cols] * fade + jnp.dot(
            weights.astype(jnp.bfloat16), v_ref[:, cols], preferred_element_type=jnp.float32
        )
        out_ref[:, width + h : width + h + 1] = peak
        out_ref[:, width + STATS + h : width + STATS + h + 1] = total


def _attention_call(kernel, query, keys, values, state):
    count, width = query.shape
    size = width // HEADS
    body = lambda *refs: kernel(*refs, size=size, scale=1.0 / math.sqrt(size))
    shapes = [
        jax.ShapeDtypeStruct((count, width), jnp.float32),
        jax.ShapeDtypeStruct((count, HEADS), jnp.float32),
        jax.ShapeDtypeStruct((count, HEADS), jnp.float32),
    ]
    return pl.pallas_call(
        body,
        out_shape=shapes,
        compiler_params=pltpu.CompilerParams(vmem_limit_bytes=48 * 1024 * 1024),
    )(query, keys, values, *state)


def final_kernel(q_ref, k_ref, v_ref, o1_ref, m1_ref, l1_ref, t_ref, out_ref, *, size, rows):
    width = HEADS * size
    for h in range(HEADS):
        cols = slice(h * size, (h + 1) * size)
        scores = lax.dot_general(
            q_ref[rows, cols], k_ref[:, cols], (((1,), (1,)), ((), ())),
            preferred_element_type=jnp.float32,
        )
        before = m1_ref[rows, h : h + 1]
        theirs = t_ref[:, width + h : width + h + 1]
        top = jnp.maximum(jnp.maximum(before, theirs), jnp.max(scores, axis=1, keepdims=True))
        weights = jnp.exp(scores - top)
        fade, their_fade = jnp.exp(before - top), jnp.exp(theirs - top)
        total = (
            l1_ref[rows, h : h + 1] * fade
            + t_ref[:, width + STATS + h : width + STATS + h + 1] * their_fade
            + jnp.sum(weights, axis=1, keepdims=True)
        )
        summed = (
            o1_ref[rows, cols] * fade
            + t_ref[:, cols] * their_fade
            + jnp.dot(weights.astype(jnp.bfloat16), v_ref[:, cols], preferred_element_type=jnp.float32)
        )
        out_ref[:, cols] = (summed / total).astype(out_ref.dtype)


def _whole(array):
    return pl.BlockSpec(array.shape, lambda i: (0,) * array.ndim)


def _row_specs(query, keys, start, count):
    block = start // count
    width = query.shape[1]
    rows = lambda cols: pl.BlockSpec((count, cols), lambda i: (block, 0))
    return [rows(width), _whole(keys), _whole(keys), rows(width), rows(HEADS), rows(HEADS)]


def spatial_final(query, keys, values, state, theirs, start, count):
    width = query.shape[1]
    body = lambda *refs: final_kernel(
        *refs, size=width // HEADS, rows=slice(None)
    )
    return pl.pallas_call(
        body,
        grid=(1,),
        in_specs=_row_specs(query, keys, start, count) + [_whole(theirs)],
        out_specs=pl.BlockSpec((count, width), lambda i: (0, 0)),
        out_shape=jax.ShapeDtypeStruct((count, width), jnp.bfloat16),
        compiler_params=pltpu.CompilerParams(vmem_limit_bytes=48 * 1024 * 1024),
    )(query, keys, values, *state, theirs)


def spatial_partial(query, keys, values):
    return _attention_call(partial_kernel, query, keys, values, ())


def spatial_merge(query, keys, values, state, start, count):
    width = query.shape[1]
    size = width // HEADS
    body = lambda *refs: merge_kernel(*refs, size=size, rows=slice(None))
    return pl.pallas_call(
        body,
        grid=(1,),
        in_specs=_row_specs(query, keys, start, count),
        out_specs=pl.BlockSpec((count, width + 2 * STATS), lambda i: (0, 0)),
        out_shape=jax.ShapeDtypeStruct((count, width + 2 * STATS), jnp.float32),
        compiler_params=pltpu.CompilerParams(vmem_limit_bytes=48 * 1024 * 1024),
    )(query, keys, values, *state)


def spread_y(rows):
    ring = lax.axis_size("y")
    pieces = [rows]
    for shift in sorted(range(1, ring), key=lambda s: -min(s, ring - s)):
        pairs = [(i, (i + shift) % ring) for i in range(ring)]
        pieces.append(lax.ppermute(rows, "y", pairs))
    return pieces


def attend_cells(block_qkv):
    cells, frames = (block_qkv.shape[0], block_qkv.shape[1])
    width = block_qkv.shape[2] // 3
    size = width // HEADS
    query = block_qkv[:, :, :width].reshape(cells, frames, HEADS, size)
    keys = block_qkv[:, :, width : 2 * width].reshape(cells, frames, HEADS, size)
    values = block_qkv[:, :, 2 * width :].reshape(cells, frames, HEADS, size)
    scores = jnp.einsum("cfhe,cghe->chfg", query, keys, preferred_element_type=jnp.float32)
    later = jnp.arange(frames)[:, None] >= jnp.arange(frames)[None, :]
    scores = jnp.where(later, scores, -1e30)
    peak = jnp.max(scores, axis=3, keepdims=True)
    weights = jnp.exp(scores - peak)
    total = jnp.sum(weights, axis=3)
    summed = jnp.einsum(
        "chfg,cghe->cfhe", weights.astype(jnp.bfloat16), values, preferred_element_type=jnp.float32
    )
    context = summed / jnp.transpose(total, (0, 2, 1))[..., None]
    return context.reshape(cells, frames, width).astype(jnp.bfloat16)


def layer(
    tokens, norm_spatial, w_spatial, w_spatial_out, norm_temporal, w_temporal, w_temporal_out
):
    frames_here, rows, width = tokens.shape
    count = frames_here * rows
    resid = tokens.reshape(count, width).astype(jnp.float32)
    normed = layer_norm(resid, norm_spatial).astype(jnp.bfloat16)
    w_query = w_spatial[:, :width] * jnp.asarray(1.0 / math.sqrt(width // HEADS), w_spatial.dtype)
    query = jnp.dot(normed, w_query, preferred_element_type=jnp.float32).astype(jnp.bfloat16)
    partner = lax.ppermute(normed, "zhi", [(0, 1), (1, 0)])
    swap = [(0, 1), (1, 0)]
    both = jnp.concatenate([lax.ppermute(query, "core", swap), query], axis=0)
    w_pairs = w_spatial[:, width:]
    near_pieces = spread_y(normed)
    far_pieces = spread_y(partner)
    near_rows = jnp.concatenate(near_pieces + [partner], axis=0)
    far_rows = jnp.concatenate(far_pieces[1:], axis=0)
    near = jnp.dot(near_rows, w_pairs, preferred_element_type=jnp.float32).astype(jnp.bfloat16)
    state = spatial_partial(both, near[:, :width], near[:, width:])
    far = jnp.dot(far_rows, w_pairs, preferred_element_type=jnp.float32).astype(jnp.bfloat16)
    theirs = spatial_merge(both, far[:, :width], far[:, width:], state, 0, count)
    theirs = lax.ppermute(theirs, "core", swap)
    context = spatial_final(both, far[:, :width], far[:, width:], state, theirs, count, count)
    after = resid + jnp.dot(context, w_spatial_out, preferred_element_type=jnp.float32)
    second = layer_norm(after, norm_temporal).astype(jnp.bfloat16)
    owners = lax.axis_size(("x", "zlo"))
    share = rows // owners
    second = second.reshape(owners, share, frames_here, width)
    gathered = lax.all_to_all(second, ("x", "zlo"), split_axis=0, concat_axis=2, tiled=True)
    frames_all = gathered.shape[2]
    w_temporal = w_temporal.at[:, :width].multiply(
        jnp.asarray(1.0 / math.sqrt(width // HEADS), w_temporal.dtype)
    )
    qkv_t = jnp.dot(
        gathered.reshape(share * frames_all, width), w_temporal, preferred_element_type=jnp.float32
    ).astype(jnp.bfloat16)
    context_t = attend_cells(qkv_t.reshape(share, frames_all, 3 * width))
    returned = lax.all_to_all(context_t, ("x", "zlo"), split_axis=1, concat_axis=0, tiled=True)
    mixed = after + jnp.dot(
        returned.reshape(count, width), w_temporal_out, preferred_element_type=jnp.float32
    )
    return mixed.reshape(frames_here, rows, width).astype(jnp.bfloat16)


def solution(mesh):
    frame_n, row_n = mesh.devices.shape
    devices = mesh.devices.reshape(4, frame_n // 4, row_n // 4, 2, 2)
    fine = Mesh(devices, ("x", "zlo", "y", "zhi", "core"))
    grid_spec = P(("x", "zlo"), ("y", "zhi", "core"), None)
    in_specs = (grid_spec, P(), P(), P(), P(), P(), P())
    return jax.shard_map(layer, mesh=fine, in_specs=in_specs, out_specs=grid_spec, check_vma=False)
```

profile of v0, /device:TPU:1, one launch (start us, length us, event | category | flops | bytes accessed | tf_op | source)
XLA Modules:
  0.0 147.5 jit_solution(8802505625621002451)
XLA Ops:
  0.0 0.0 copy-start
  0.0 0.0 copy-start.5
  0.0 0.0 copy-start.7
  0.0 1.0 copy-done.2
  1.0 0.1 convert_reduce_fusion
  1.1 0.2 fusion.16
  1.4 0.0 copy-done.5
  1.4 0.1 constant_dynamic-update-slice_fusion.4
  1.5 5.6 %collective-permute-start.5 = (bf16[256,512]{1,0:T(8,128)(2,1)S(1)}, bf16[256,512]{1,0:T(8,128)(2,1)S(1)}, u32[]{:S(2)}, u32[]{:S(2)}) collective-permute-start(bf16[256,512]{1,0:T(8,128)(2,1)S(1)} %get-tuple-element.24), channel_id=1, source_target_pairs={{0,8},{4,12},{8,0},{12,4},{1,9},{5,13},{9,1},{13,5},{2,10},{6,14},... | collective-permute-start | bytes 786440 | tf_op jit(solution)/shard_map/ppermute | solution.py:155
  7.2 2.3 %collective-permute-start.6 = (bf16[256,512]{1,0:T(8,128)(2,1)S(1)}, bf16[256,512]{1,0:T(8,128)(2,1)S(1)}, u32[]{:S(2)}, u32[]{:S(2)}) collective-permute-start(bf16[256,512]{1,0:T(8,128)(2,1)S(1)} %get-tuple-element.24), channel_id=1, source_target_pairs={{0,4},{4,8},{8,12},{12,0},{1,5},{5,9},{9,13},{13,1},{2,6},{6,10},{... | collective-permute-start | bytes 786440 | tf_op jit(solution)/shard_map/ppermute | solution.py:155
  9.5 4.2 %collective-permute-start.7 = (bf16[256,512]{1,0:T(8,128)(2,1)S(1)}, bf16[256,512]{1,0:T(8,128)(2,1)S(1)}, u32[]{:S(2)}, u32[]{:S(2)}) collective-permute-start(bf16[256,512]{1,0:T(8,128)(2,1)S(1)} %get-tuple-element.24), channel_id=1, source_target_pairs={{0,12},{4,0},{8,4},{12,8},{1,13},{5,1},{9,5},{13,9},{2,14},{6,2},{... | collective-permute-start | bytes 786440 | tf_op jit(solution)/shard_map/ppermute | solution.py:155
  13.7 15.4 %collective-permute-start.1 = (bf16[256,512]{1,0:T(8,128)(2,1)S(1)}, bf16[256,512]{1,0:T(8,128)(2,1)S(1)}, u32[]{:S(2)}, u32[]{:S(2)}) collective-permute-start(bf16[256,512]{1,0:T(8,128)(2,1)S(1)} %get-tuple-element.24), channel_id=1, source_target_pairs={{0,2},{2,0},{1,3},{3,1},{4,6},{6,4},{5,7},{7,5},{8,10},{10,8},{9,1... | collective-permute-start | bytes 786440 | tf_op jit(solution)/shard_map/ppermute | solution.py:188
  29.1 0.0 copy-done.7
  29.1 0.3 convolution_convert_fusion.3
  29.5 3.7 %collective-permute-start = (bf16[256,512]{1,0:T(8,128)(2,1)S(1)}, bf16[256,512]{1,0:T(8,128)(2,1)S(1)}, u32[]{:S(2)}, u32[]{:S(2)}) collective-permute-start(bf16[256,512]{1,0:T(8,128)(2,1)S(1)} %convolution_convert_fusion.3), channel_id=1, source_target_pairs={{0,1},{1,0},{2,3},{3,2},{4,5},{5,4},{6,7},{7,6},{8,9},{9,8},{10,11... | collective-permute-start | bytes 786440 | tf_op jit(solution)/shard_map/ppermute | solution.py:190
  33.2 0.0 collective-permute-done.5
  33.2 0.0 collective-permute-done.6
  33.2 0.0 collective-permute-done.7
  33.3 1.0 collective-permute-done.1
  34.3 1.5 %convolution_convert_fusion = bf16[1280,1024]{1,0:T(8,128)(2,1)S(1)} fusion(bf16[1280,512]{1,0:T(8,128)(2,1)S(1)} %constant_dynamic-update-slice_fusion, bf16[512,1536]{1,0:T(8,128)(2,1)S(1)} %copy-done.7), kind=kOutput, calls=%fused_computation | convolution fusion | flops 1343488000 | bytes 4980736 | tf_op jit(solution)/shard_map/dot_general | solution.py:196
  35.8 1.9 %collective-permute-start.2 = (bf16[256,512]{1,0:T(8,128)(2,1)S(1)}, bf16[256,512]{1,0:T(8,128)(2,1)S(1)}, u32[]{:S(2)}, u32[]{:S(2)}) collective-permute-start(bf16[256,512]{1,0:T(8,128)(2,1)S(1)} %collective-permute-done.1), channel_id=1, source_target_pairs={{0,8},{4,12},{8,0},{12,4},{1,9},{5,13},{9,1},{13,5},{2,10},{6,14},... | collective-permute-start | bytes 786440 | tf_op jit(solution)/shard_map/ppermute | solution.py:155
  37.8 2.8 %collective-permute-start.3 = (bf16[256,512]{1,0:T(8,128)(2,1)S(1)}, bf16[256,512]{1,0:T(8,128)(2,1)S(1)}, u32[]{:S(2)}, u32[]{:S(2)}) collective-permute-start(bf16[256,512]{1,0:T(8,128)(2,1)S(1)} %collective-permute-done.1), channel_id=1, source_target_pairs={{0,4},{4,8},{8,12},{12,0},{1,5},{5,9},{9,13},{13,1},{2,6},{6,10},{... | collective-permute-start | bytes 786440 | tf_op jit(solution)/shard_map/ppermute | solution.py:155
  40.5 3.9 %collective-permute-start.4 = (bf16[256,512]{1,0:T(8,128)(2,1)S(1)}, bf16[256,512]{1,0:T(8,128)(2,1)S(1)}, u32[]{:S(2)}, u32[]{:S(2)}) collective-permute-start(bf16[256,512]{1,0:T(8,128)(2,1)S(1)} %collective-permute-done.1), channel_id=1, source_target_pairs={{0,12},{4,0},{8,4},{12,8},{1,13},{5,1},{9,5},{13,9},{2,14},{6,2},{... | collective-permute-start | bytes 786440 | tf_op jit(solution)/shard_map/ppermute | solution.py:155
  44.5 0.2 fusion.33
  44.7 0.0 collective-permute-done
  44.7 7.3 %shard_map.73 = (f32[512,512]{1,0:T(8,128)S(1)}, f32[512,8]{1,0:T(8,128)S(1)}, f32[512,8]{1,0:T(8,128)S(1)}) custom-call(bf16[512,512]{1,0:T(8,128)(2,1)S(1)} %pad_maximum_fusion.refs_0_, bf16[1280,512]{1,0:T(8,128)(2,1)S(1)} %get-tuple-element.26.refs_1_, bf16[1280,512]{1,0:T(8,128)(2,1)S(1)} %get-tuple-element.25.refs_2_), custom_call_target="tpu_custom_call" | custom-call | tf_op jit(solution)/shard_map/pallas_call | solution.py:73
  52.0 0.0 collective-permute-done.2
  52.0 0.2 collective-permute-done.3
  52.2 0.0 collective-permute-done.4
  52.2 1.0 convolution_convert_fusion.2
  53.2 0.1 fusion.34
  53.3 4.7 %shard_map.74 = f32[256,640]{1,0:T(8,128)S(1)} custom-call(bf16[512,512]{1,0:T(8,128)(2,1)S(1)} %pad_maximum_fusion.refs_0_, bf16[768,512]{1,0:T(8,128)(2,1)S(1)} %get-tuple-element.28.refs_1_, bf16[768,512]{1,0:T(8,128)(2,1)S(1)} %get-tuple-element.27.refs_2_, f32[512,512]{1,0:T(8,128)S(1)} %get-tuple-element.20.refs_3_, ...), custom_call_target="tpu_custom_call" | custom-call | tf_op jit(solution)/shard_map/pallas_call | solution.py:140
  58.0 4.8 %collective-permute-start.8 = (f32[256,640]{1,0:T(8,128)S(1)}, f32[256,640]{1,0:T(8,128)S(1)}, u32[]{:S(2)}, u32[]{:S(2)}) collective-permute-start(f32[256,640]{1,0:T(8,128)S(1)} %shard_map.74), channel_id=1, source_target_pairs={{0,1},{1,0},{2,3},{3,2},{4,5},{5,4},{6,7},{7,6},{8,9},{9,8},{10,11... | collective-permute-start | bytes 1966088 | tf_op jit(solution)/shard_map/ppermute | solution.py:200
  62.8 1.7 %collective-permute-done.8.refs_6_ = f32[256,640]{1,0:T(8,128)S(1)} collective-permute-done((f32[256,640]{1,0:T(8,128)S(1)}, f32[256,640]{1,0:T(8,128)S(1)}, u32[]{:S(2)}, u32[]{:S(2)}) %collective-permute-start.8) | collective-permute-done | bytes 655392 | tf_op jit(solution)/shard_map/ppermute | solution.py:200
  64.5 6.8 %shard_map.75 = bf16[256,512]{1,0:T(8,128)(2,1)S(1)} custom-call(bf16[512,512]{1,0:T(8,128)(2,1)S(1)} %pad_maximum_fusion.refs_0_, bf16[768,512]{1,0:T(8,128)(2,1)S(1)} %get-tuple-element.28.refs_1_, bf16[768,512]{1,0:T(8,128)(2,1)S(1)} %get-tuple-element.27.refs_2_, f32[512,512]{1,0:T(8,128)S(1)} %get-tuple-element.20.refs_3_, ...), custom_call_target="tpu_custom_call" | custom-call | tf_op jit(solution)/shard_map/pallas_call | solution.py:122
  71.4 0.0 copy-done
  71.4 0.0 copy-start.6
  71.4 0.0 copy-start.1
  71.4 0.4 fusion.36
  71.8 0.2 multiply_reduce_fusion
  72.0 0.0 copy-done.6
  72.1 0.9 fusion.27
  72.9 26.3 %all-to-all-start = ((bf16[32,8,1,512]{3,1,2,0:T(8,128)(2,1)}), bf16[32,8,1,512]{3,1,2,0:T(8,128)(2,1)S(1)}, u32[]{:S(2)}, u32[]{:S(2)}) async-start(bf16[32,8,1,512]{3,1,2,0:T(8,128)(2,1)} %fusion.27), calls=%async_computation | async-start | bytes 524288 | tf_op jit(solution)/shard_map/all_to_all | solution.py:207
  99.3 0.6 compare_reduce_fusion
  99.9 0.0 copy-done.1
  99.9 0.7 fusion.19
  100.6 17.4 %all-to-all-done = bf16[32,8,1,512]{3,1,2,0:T(8,128)(2,1)S(1)} async-done(((bf16[32,8,1,512]{3,1,2,0:T(8,128)(2,1)}), bf16[32,8,1,512]{3,1,2,0:T(8,128)(2,1)S(1)}, u32[]{:S(2)}, u32[]{:S(2)}) %all-to-all-start) | async-done | bytes 262176 | tf_op jit(solution)/shard_map/all_to_all | solution.py:207
  118.1 0.1 copy.17
  118.2 0.6 convolution_convert_fusion.1
  118.7 0.1 fusion.35
  118.8 0.3 reshape.85
  119.1 0.3 reshape.86
  119.4 1.1 reshape.84
  120.5 0.0 copy-start.4
  120.5 0.4 fusion.37
  120.9 0.3 fusion.4
  121.1 0.3 copy-done.4
  121.5 0.6 fusion.1
  122.1 0.0 copy-start.3
  122.1 0.2 copy.25
  122.3 0.3 reshape.88
  122.6 23.9 %all_to_all.30 = bf16[8,32,512]{2,0,1:T(8,128)(2,1)S(1)} all-to-all(bf16[8,32,512]{2,0,1:T(8,128)(2,1)S(1)} %reshape.88), channel_id=1, replica_groups=mesh['x'=4,'zlo'=8,'y'=4,'zhi'=2,'core'=2] {'x','zlo'}, dimensions={1} | all-to-all | bytes 524288 | tf_op jit(solution)/shard_map/all_to_all | solution.py:216
  146.5 0.0 copy-done.3
  146.5 1.0 fusion.3
  (11 shorter events, 0.1 us)
Async XLA Ops:
  0.0 71.4 %copy-start = (bf16[512,512]{1,0:T(8,128)(2,1)S(1)}, bf16[512,512]{1,0:T(8,128)(2,1)}, u32[]{:S(2)}) copy-start(bf16[512,512]{1,0:T(8,128)(2,1)} %param.12) | copy-start | bytes 1572868
  0.0 1.0 copy-start.2
  0.0 1.4 copy-start.5
  0.0 29.1 %copy-start.7 = (bf16[512,1536]{1,0:T(8,128)(2,1)S(1)}, bf16[512,1536]{1,0:T(8,128)(2,1)}, u32[]{:S(2)}) copy-start(bf16[512,1536]{1,0:T(8,128)(2,1)} %param.11) | copy-start | bytes 4718596
  1.5 31.6 %collective-permute-start.5 = (bf16[256,512]{1,0:T(8,128)(2,1)S(1)}, bf16[256,512]{1,0:T(8,128)(2,1)S(1)}, u32[]{:S(2)}, u32[]{:S(2)}) collective-permute-start(bf16[256,512]{1,0:T(8,128)(2,1)S(1)} %get-tuple-element.24), channel_id=1, source_target_pairs={{0,8},{4,12},{8,0},{12,4},{1,9},{5,13},{9,1},{13,5},{2,10},{6,14},... | collective-permute-start | bytes 786440 | tf_op jit(solution)/shard_map/ppermute | solution.py:155
  7.2 26.0 %collective-permute-start.6 = (bf16[256,512]{1,0:T(8,128)(2,1)S(1)}, bf16[256,512]{1,0:T(8,128)(2,1)S(1)}, u32[]{:S(2)}, u32[]{:S(2)}) collective-permute-start(bf16[256,512]{1,0:T(8,128)(2,1)S(1)} %get-tuple-element.24), channel_id=1, source_target_pairs={{0,4},{4,8},{8,12},{12,0},{1,5},{5,9},{9,13},{13,1},{2,6},{6,10},{... | collective-permute-start | bytes 786440 | tf_op jit(solution)/shard_map/ppermute | solution.py:155
  9.5 23.8 %collective-permute-start.7 = (bf16[256,512]{1,0:T(8,128)(2,1)S(1)}, bf16[256,512]{1,0:T(8,128)(2,1)S(1)}, u32[]{:S(2)}, u32[]{:S(2)}) collective-permute-start(bf16[256,512]{1,0:T(8,128)(2,1)S(1)} %get-tuple-element.24), channel_id=1, source_target_pairs={{0,12},{4,0},{8,4},{12,8},{1,13},{5,1},{9,5},{13,9},{2,14},{6,2},{... | collective-permute-start | bytes 786440 | tf_op jit(solution)/shard_map/ppermute | solution.py:155
  13.7 20.6 %collective-permute-start.1 = (bf16[256,512]{1,0:T(8,128)(2,1)S(1)}, bf16[256,512]{1,0:T(8,128)(2,1)S(1)}, u32[]{:S(2)}, u32[]{:S(2)}) collective-permute-start(bf16[256,512]{1,0:T(8,128)(2,1)S(1)} %get-tuple-element.24), channel_id=1, source_target_pairs={{0,2},{2,0},{1,3},{3,1},{4,6},{6,4},{5,7},{7,5},{8,10},{10,8},{9,1... | collective-permute-start | bytes 786440 | tf_op jit(solution)/shard_map/ppermute | solution.py:188
  29.5 15.2 %collective-permute-start = (bf16[256,512]{1,0:T(8,128)(2,1)S(1)}, bf16[256,512]{1,0:T(8,128)(2,1)S(1)}, u32[]{:S(2)}, u32[]{:S(2)}) collective-permute-start(bf16[256,512]{1,0:T(8,128)(2,1)S(1)} %convolution_convert_fusion.3), channel_id=1, source_target_pairs={{0,1},{1,0},{2,3},{3,2},{4,5},{5,4},{6,7},{7,6},{8,9},{9,8},{10,11... | collective-permute-start | bytes 786440 | tf_op jit(solution)/shard_map/ppermute | solution.py:190
  35.8 16.1 %collective-permute-start.2 = (bf16[256,512]{1,0:T(8,128)(2,1)S(1)}, bf16[256,512]{1,0:T(8,128)(2,1)S(1)}, u32[]{:S(2)}, u32[]{:S(2)}) collective-permute-start(bf16[256,512]{1,0:T(8,128)(2,1)S(1)} %collective-permute-done.1), channel_id=1, source_target_pairs={{0,8},{4,12},{8,0},{12,4},{1,9},{5,13},{9,1},{13,5},{2,10},{6,14},... | collective-permute-start | bytes 786440 | tf_op jit(solution)/shard_map/ppermute | solution.py:155
  37.8 14.5 %collective-permute-start.3 = (bf16[256,512]{1,0:T(8,128)(2,1)S(1)}, bf16[256,512]{1,0:T(8,128)(2,1)S(1)}, u32[]{:S(2)}, u32[]{:S(2)}) collective-permute-start(bf16[256,512]{1,0:T(8,128)(2,1)S(1)} %collective-permute-done.1), channel_id=1, source_target_pairs={{0,4},{4,8},{8,12},{12,0},{1,5},{5,9},{9,13},{13,1},{2,6},{6,10},{... | collective-permute-start | bytes 786440 | tf_op jit(solution)/shard_map/ppermute | solution.py:155
  40.5 11.7 %collective-permute-start.4 = (bf16[256,512]{1,0:T(8,128)(2,1)S(1)}, bf16[256,512]{1,0:T(8,128)(2,1)S(1)}, u32[]{:S(2)}, u32[]{:S(2)}) collective-permute-start(bf16[256,512]{1,0:T(8,128)(2,1)S(1)} %collective-permute-done.1), channel_id=1, source_target_pairs={{0,12},{4,0},{8,4},{12,8},{1,13},{5,1},{9,5},{13,9},{2,14},{6,2},{... | collective-permute-start | bytes 786440 | tf_op jit(solution)/shard_map/ppermute | solution.py:155
  58.0 6.5 %collective-permute-start.8 = (f32[256,640]{1,0:T(8,128)S(1)}, f32[256,640]{1,0:T(8,128)S(1)}, u32[]{:S(2)}, u32[]{:S(2)}) collective-permute-start(f32[256,640]{1,0:T(8,128)S(1)} %shard_map.74), channel_id=1, source_target_pairs={{0,1},{1,0},{2,3},{3,2},{4,5},{5,4},{6,7},{7,6},{8,9},{9,8},{10,11... | collective-permute-start | bytes 1966088 | tf_op jit(solution)/shard_map/ppermute | solution.py:200
  71.4 0.7 copy-start.6
  71.4 28.5 %copy-start.1 = (bf16[512,1536]{1,0:T(8,128)(2,1)S(1)}, bf16[512,1536]{1,0:T(8,128)(2,1)}, u32[]{:S(2)}) copy-start(bf16[512,1536]{1,0:T(8,128)(2,1)} %param.14) | copy-start | bytes 4718596
  72.9 45.1 %all-to-all-start = ((bf16[32,8,1,512]{3,1,2,0:T(8,128)(2,1)}), bf16[32,8,1,512]{3,1,2,0:T(8,128)(2,1)S(1)}, u32[]{:S(2)}, u32[]{:S(2)}) async-start(bf16[32,8,1,512]{3,1,2,0:T(8,128)(2,1)} %fusion.27), calls=%async_computation | async-start | bytes 524288 | tf_op jit(solution)/shard_map/all_to_all | solution.py:207
  120.5 1.0 copy-start.4
  122.1 24.4 %copy-start.3 = (bf16[512,512]{1,0:T(8,128)(2,1)S(1)}, bf16[512,512]{1,0:T(8,128)(2,1)}, u32[]{:S(2)}) copy-start(bf16[512,512]{1,0:T(8,128)(2,1)} %param.15) | copy-start | bytes 1572868
where the time goes:
time: 148 us
  starting transfers between devices  71 us (48%)
  blocking collectives  23.9 us (16%)
  waiting for transfers between devices  20.4 us (14%)
  Pallas kernels  18.8 us (13%)
  matrix products  5.73 us (4%)
  local copies, waits for them, and re-layouts  4.11 us (3%)
  other arithmetic  3.21 us (2%)
    all_to_all x1, starting transfers between devices, layer(): lax.all_to_all(second, ('x', 'zlo'), split_axis=0, concat_axis=2, tiled=T...  26.3 us
    all_to_all x1, blocking collectives, layer(): lax.all_to_all(context_t, ('x', 'zlo'), split_axis=1, concat_axis=0, tile...  23.9 us
    ppermute x6, starting transfers between devices, spread_y(): pieces.append(lax.ppermute(rows, 'y', pairs))  20.7 us
    all_to_all x1, waiting for transfers between devices, layer(): lax.all_to_all(second, ('x', 'zlo'), split_axis=0, concat_axis=2, tiled=T...  17.4 us
    ppermute x1, starting transfers between devices, layer(): partner = lax.ppermute(normed, 'zhi', [(0, 1), (1, 0)])  15.4 us
    pallas_call x1, Pallas kernels, _attention_call(): pl.pallas_call(body, out_shape=shapes, compiler_params=pltpu.CompilerPara...  7.25 us
    pallas_call x1, Pallas kernels, spatial_final(): pl.pallas_call(body, grid=(1,), in_specs=_row_specs(query, keys, start, c...  6.82 us
    ppermute x1, starting transfers between devices, layer(): theirs = lax.ppermute(theirs, 'core', swap)  4.82 us
  transfers between devices with their start and end apart: 10, of which 4 were waited for; matrix products, arithmetic and copies ran while one was open for 2% of the time, Pallas kernels for 5%

commit v1 on v0

--- a/solution.py
+++ b/solution.py
@@ -153,7 +153,7 @@
     for shift in sorted(range(1, ring), key=lambda s: -min(s, ring - s)):
         pairs = [(i, (i + shift) % ring) for i in range(ring)]
         pieces.append(lax.ppermute(rows, "y", pairs))
-    return pieces
+    return jnp.concatenate(pieces, axis=0)
 
 
 def attend_cells(block_qkv):
@@ -189,12 +189,10 @@
     swap = [(0, 1), (1, 0)]
     both = jnp.concatenate([lax.ppermute(query, "core", swap), query], axis=0)
     w_pairs = w_spatial[:, width:]
-    near_pieces = spread_y(normed)
-    far_pieces = spread_y(partner)
-    near_rows = jnp.concatenate(near_pieces + [partner], axis=0)
-    far_rows = jnp.concatenate(far_pieces[1:], axis=0)
+    near_rows = spread_y(normed)
     near = jnp.dot(near_rows, w_pairs, preferred_element_type=jnp.float32).astype(jnp.bfloat16)
     state = spatial_partial(both, near[:, :width], near[:, width:])
+    far_rows = spread_y(partner)
     far = jnp.dot(far_rows, w_pairs, preferred_element_type=jnp.float32).astype(jnp.bfloat16)
     theirs = spatial_merge(both, far[:, :width], far[:, width:], state, 0, count)
     theirs = lax.ppermute(theirs, "core", swap)

time: 148 us -> 139 us (0.939)
  starting transfers between devices: 71 us -> 62.5 us
    all_to_all x1, starting transfers between devices: 26.3 us -> 18.8 us  [layer(): lax.all_to_all(second, ('x', 'zlo'), split_axis=0, concat_axis=2, tiled=T...]
  transfers between devices with their start and end apart: 10 -> 10, of which waited for: 4 -> 3; matrix products, arithmetic and copies ran while one was open for 2% -> 2% of each run, Pallas kernels for 5% -> 4%
where the time goes in v1:
time: 139 us
  starting transfers between devices  62.5 us (45%)
  blocking collectives  23.9 us (17%)
  waiting for transfers between devices  20.3 us (15%)
  Pallas kernels  18.4 us (13%)
  matrix products  5.74 us (4%)
  local copies, waits for them, and re-layouts  4.05 us (3%)
  other arithmetic  3.28 us (2%)
    all_to_all x1, blocking collectives, layer(): lax.all_to_all(context_t, ('x', 'zlo'), split_axis=1, concat_axis=0, tile...  23.9 us
    ppermute x6, starting transfers between devices, spread_y(): pieces.append(lax.ppermute(rows, 'y', pairs))  19.7 us
    all_to_all x1, starting transfers between devices, layer(): lax.all_to_all(second, ('x', 'zlo'), split_axis=0, concat_axis=2, tiled=T...  18.8 us
    all_to_all x1, waiting for transfers between devices, layer(): lax.all_to_all(second, ('x', 'zlo'), split_axis=0, concat_axis=2, tiled=T...  17.4 us
    ppermute x1, starting transfers between devices, layer(): partner = lax.ppermute(normed, 'zhi', [(0, 1), (1, 0)])  16.3 us
    pallas_call x1, Pallas kernels, spatial_final(): pl.pallas_call(body, grid=(1,), in_specs=_row_specs(query, keys, start, c...  7.09 us
    pallas_call x1, Pallas kernels, _attention_call(): pl.pallas_call(body, out_shape=shapes, compiler_params=pltpu.CompilerPara...  6.07 us
    pallas_call x1, Pallas kernels, spatial_merge(): pl.pallas_call(body, grid=(1,), in_specs=_row_specs(query, keys, start, c...  5.25 us
  transfers between devices with their start and end apart: 10, of which 3 were waited for; matrix products, arithmetic and copies ran while one was open for 2% of the time, Pallas kernels for 4%

profile of v1, /device:TPU:1, one launch (start us, length us, event | category | flops | bytes accessed | tf_op | source)
XLA Modules:
  0.0 138.5 jit_solution(18339163631089204902)
XLA Ops:
  0.0 0.0 copy-start
  0.0 0.0 copy-start.5
  0.0 0.0 copy-start.7
  0.0 1.0 copy-done.2
  1.0 0.1 convert_reduce_fusion
  1.1 0.2 fusion.25
  1.4 0.0 copy-done.5
  1.4 0.1 fusion.27
  1.5 16.3 %collective-permute-start.1 = (bf16[256,512]{1,0:T(8,128)(2,1)S(1)}, bf16[256,512]{1,0:T(8,128)(2,1)S(1)}, u32[]{:S(2)}, u32[]{:S(2)}) collective-permute-start(bf16[256,512]{1,0:T(8,128)(2,1)S(1)} %fusion.27), channel_id=1, source_target_pairs={{0,2},{2,0},{1,3},{3,1},{4,6},{6,4},{5,7},{7,5},{8,10},{10,8},{9,1... | collective-permute-start | bytes 786440 | tf_op jit(solution)/shard_map/ppermute | solution.py:188
  17.8 0.0 copy-done.7
  17.8 0.3 convolution_convert_fusion.3
  18.1 2.9 %collective-permute-start = (bf16[256,512]{1,0:T(8,128)(2,1)S(1)}, bf16[256,512]{1,0:T(8,128)(2,1)S(1)}, u32[]{:S(2)}, u32[]{:S(2)}) collective-permute-start(bf16[256,512]{1,0:T(8,128)(2,1)S(1)} %convolution_convert_fusion.3), channel_id=1, source_target_pairs={{0,1},{1,0},{2,3},{3,2},{4,5},{5,4},{6,7},{7,6},{8,9},{9,8},{10,11... | collective-permute-start | bytes 786440 | tf_op jit(solution)/shard_map/ppermute | solution.py:190
  21.0 4.8 %collective-permute-start.5 = (bf16[256,512]{1,0:T(8,128)(2,1)S(1)}, bf16[256,512]{1,0:T(8,128)(2,1)S(1)}, u32[]{:S(2)}, u32[]{:S(2)}) collective-permute-start(bf16[256,512]{1,0:T(8,128)(2,1)S(1)} %fusion.27), channel_id=1, source_target_pairs={{0,8},{4,12},{8,0},{12,4},{1,9},{5,13},{9,1},{13,5},{2,10},{6,14},... | collective-permute-start | bytes 786440 | tf_op jit(solution)/shard_map/ppermute | solution.py:155
  25.8 2.3 %collective-permute-start.6 = (bf16[256,512]{1,0:T(8,128)(2,1)S(1)}, bf16[256,512]{1,0:T(8,128)(2,1)S(1)}, u32[]{:S(2)}, u32[]{:S(2)}) collective-permute-start(bf16[256,512]{1,0:T(8,128)(2,1)S(1)} %fusion.27), channel_id=1, source_target_pairs={{0,4},{4,8},{8,12},{12,0},{1,5},{5,9},{9,13},{13,1},{2,6},{6,10},{... | collective-permute-start | bytes 786440 | tf_op jit(solution)/shard_map/ppermute | solution.py:155
  28.1 4.2 %collective-permute-start.7 = (bf16[256,512]{1,0:T(8,128)(2,1)S(1)}, bf16[256,512]{1,0:T(8,128)(2,1)S(1)}, u32[]{:S(2)}, u32[]{:S(2)}) collective-permute-start(bf16[256,512]{1,0:T(8,128)(2,1)S(1)} %fusion.27), channel_id=1, source_target_pairs={{0,12},{4,0},{8,4},{12,8},{1,13},{5,1},{9,5},{13,9},{2,14},{6,2},{... | collective-permute-start | bytes 786440 | tf_op jit(solution)/shard_map/ppermute | solution.py:155
  32.3 0.0 collective-permute-done.1
  32.3 1.9 %collective-permute-start.2 = (bf16[256,512]{1,0:T(8,128)(2,1)S(1)}, bf16[256,512]{1,0:T(8,128)(2,1)S(1)}, u32[]{:S(2)}, u32[]{:S(2)}) collective-permute-start(bf16[256,512]{1,0:T(8,128)(2,1)S(1)} %collective-permute-done.1), channel_id=1, source_target_pairs={{0,8},{4,12},{8,0},{12,4},{1,9},{5,13},{9,1},{13,5},{2,10},{6,14},... | collective-permute-start | bytes 786440 | tf_op jit(solution)/shard_map/ppermute | solution.py:155
  34.3 0.0 collective-permute-done
  34.3 2.5 %collective-permute-start.3 = (bf16[256,512]{1,0:T(8,128)(2,1)S(1)}, bf16[256,512]{1,0:T(8,128)(2,1)S(1)}, u32[]{:S(2)}, u32[]{:S(2)}) collective-permute-start(bf16[256,512]{1,0:T(8,128)(2,1)S(1)} %collective-permute-done.1), channel_id=1, source_target_pairs={{0,4},{4,8},{8,12},{12,0},{1,5},{5,9},{9,13},{13,1},{2,6},{6,10},{... | collective-permute-start | bytes 786440 | tf_op jit(solution)/shard_map/ppermute | solution.py:155
  36.8 0.0 collective-permute-done.5
  36.8 4.0 %collective-permute-start.4 = (bf16[256,512]{1,0:T(8,128)(2,1)S(1)}, bf16[256,512]{1,0:T(8,128)(2,1)S(1)}, u32[]{:S(2)}, u32[]{:S(2)}) collective-permute-start(bf16[256,512]{1,0:T(8,128)(2,1)S(1)} %collective-permute-done.1), channel_id=1, source_target_pairs={{0,12},{4,0},{8,4},{12,8},{1,13},{5,1},{9,5},{13,9},{2,14},{6,2},{... | collective-permute-start | bytes 786440 | tf_op jit(solution)/shard_map/ppermute | solution.py:155
  40.8 0.0 collective-permute-done.6
  40.9 0.0 collective-permute-done.7
  40.9 1.2 convolution_convert_fusion.1
  42.1 0.2 fusion.42
  42.3 6.1 %shard_map.73 = (f32[512,512]{1,0:T(8,128)S(1)}, f32[512,8]{1,0:T(8,128)S(1)}, f32[512,8]{1,0:T(8,128)S(1)}) custom-call(bf16[512,512]{1,0:T(8,128)(2,1)S(1)} %pad_maximum_fusion.refs_0_, bf16[1024,512]{1,0:T(8,128)(2,1)S(1)} %get-tuple-element.24.refs_1_, bf16[1024,512]{1,0:T(8,128)(2,1)S(1)} %get-tuple-element.23.refs_2_), custom_call_target="tpu_custom_call" | custom-call | tf_op jit(solution)/shard_map/pallas_call | solution.py:73
  48.4 0.0 collective-permute-done.2
  48.4 1.2 collective-permute-done.3
  49.6 0.0 collective-permute-done.4
  49.6 1.2 convolution_convert_fusion.2
  50.8 0.2 fusion.43
  51.0 5.3 %shard_map.74 = f32[256,640]{1,0:T(8,128)S(1)} custom-call(bf16[512,512]{1,0:T(8,128)(2,1)S(1)} %pad_maximum_fusion.refs_0_, bf16[1024,512]{1,0:T(8,128)(2,1)S(1)} %get-tuple-element.26.refs_1_, bf16[1024,512]{1,0:T(8,128)(2,1)S(1)} %get-tuple-element.25.refs_2_, f32[512,512]{1,0:T(8,128)S(1)} %get-tuple-element.20.refs_3_, ...), custom_call_target="tpu_custom_call" | custom-call | tf_op jit(solution)/shard_map/pallas_call | solution.py:140
  56.3 4.8 %collective-permute-start.8 = (f32[256,640]{1,0:T(8,128)S(1)}, f32[256,640]{1,0:T(8,128)S(1)}, u32[]{:S(2)}, u32[]{:S(2)}) collective-permute-start(f32[256,640]{1,0:T(8,128)S(1)} %shard_map.74), channel_id=1, source_target_pairs={{0,1},{1,0},{2,3},{3,2},{4,5},{5,4},{6,7},{7,6},{8,9},{9,8},{10,11... | collective-permute-start | bytes 1966088 | tf_op jit(solution)/shard_map/ppermute | solution.py:198
  61.1 1.7 %collective-permute-done.8.refs_6_ = f32[256,640]{1,0:T(8,128)S(1)} collective-permute-done((f32[256,640]{1,0:T(8,128)S(1)}, f32[256,640]{1,0:T(8,128)S(1)}, u32[]{:S(2)}, u32[]{:S(2)}) %collective-permute-start.8) | collective-permute-done | bytes 655392 | tf_op jit(solution)/shard_map/ppermute | solution.py:198
  62.8 7.1 %shard_map.75 = bf16[256,512]{1,0:T(8,128)(2,1)S(1)} custom-call(bf16[512,512]{1,0:T(8,128)(2,1)S(1)} %pad_maximum_fusion.refs_0_, bf16[1024,512]{1,0:T(8,128)(2,1)S(1)} %get-tuple-element.26.refs_1_, bf16[1024,512]{1,0:T(8,128)(2,1)S(1)} %get-tuple-element.25.refs_2_, f32[512,512]{1,0:T(8,128)S(1)} %get-tuple-element.20.refs_3_, ...), custom_call_target="tpu_custom_call" | custom-call | tf_op jit(solution)/shard_map/pallas_call | solution.py:122
  69.9 0.0 copy-done
  69.9 0.0 copy-start.6
  69.9 0.0 copy-start.1
  69.9 0.4 fusion.45
  70.3 0.2 multiply_reduce_fusion
  70.5 0.0 copy-done.6
  70.6 0.9 fusion.36
  71.4 18.8 %all-to-all-start = ((bf16[32,8,1,512]{3,1,2,0:T(8,128)(2,1)}), bf16[32,8,1,512]{3,1,2,0:T(8,128)(2,1)S(1)}, u32[]{:S(2)}, u32[]{:S(2)}) async-start(bf16[32,8,1,512]{3,1,2,0:T(8,128)(2,1)} %fusion.36), calls=%async_computation | async-start | bytes 524288 | tf_op jit(solution)/shard_map/all_to_all | solution.py:205
  90.3 0.6 compare_reduce_fusion
  90.9 0.0 copy-done.1
  90.9 0.8 fusion.28
  91.7 17.4 %all-to-all-done = bf16[32,8,1,512]{3,1,2,0:T(8,128)(2,1)S(1)} async-done(((bf16[32,8,1,512]{3,1,2,0:T(8,128)(2,1)}), bf16[32,8,1,512]{3,1,2,0:T(8,128)(2,1)S(1)}, u32[]{:S(2)}, u32[]{:S(2)}) %all-to-all-start) | async-done | bytes 262176 | tf_op jit(solution)/shard_map/all_to_all | solution.py:205
  109.1 0.1 copy.17
  109.2 0.6 convolution_convert_fusion
  109.7 0.1 fusion.44
  109.8 0.3 reshape.85
  110.1 0.3 reshape.86
  110.4 1.1 reshape.84
  111.5 0.0 copy-start.4
  111.5 0.4 fusion.46
  111.9 0.3 fusion.18
  112.2 0.3 copy-done.4
  112.5 0.6 fusion.1
  113.1 0.0 copy-start.3
  113.1 0.2 copy.25
  113.3 0.3 reshape.88
  113.6 23.9 %all_to_all.30 = bf16[8,32,512]{2,0,1:T(8,128)(2,1)S(1)} all-to-all(bf16[8,32,512]{2,0,1:T(8,128)(2,1)S(1)} %reshape.88), channel_id=1, replica_groups=mesh['x'=4,'zlo'=8,'y'=4,'zhi'=2,'core'=2] {'x','zlo'}, dimensions={1} | all-to-all | bytes 524288 | tf_op jit(solution)/shard_map/all_to_all | solution.py:214
  137.5 0.0 copy-done.3
  137.5 1.0 fusion.3
  (7 shorter events, 0.1 us)
Async XLA Ops:
  0.0 69.9 %copy-start = (bf16[512,512]{1,0:T(8,128)(2,1)S(1)}, bf16[512,512]{1,0:T(8,128)(2,1)}, u32[]{:S(2)}) copy-start(bf16[512,512]{1,0:T(8,128)(2,1)} %param.12) | copy-start | bytes 1572868
  0.0 1.0 copy-start.2
  0.0 1.4 copy-start.5
  0.0 17.8 %copy-start.7 = (bf16[512,1536]{1,0:T(8,128)(2,1)S(1)}, bf16[512,1536]{1,0:T(8,128)(2,1)}, u32[]{:S(2)}) copy-start(bf16[512,1536]{1,0:T(8,128)(2,1)} %param.11) | copy-start | bytes 4718596
  1.5 30.8 %collective-permute-start.1 = (bf16[256,512]{1,0:T(8,128)(2,1)S(1)}, bf16[256,512]{1,0:T(8,128)(2,1)S(1)}, u32[]{:S(2)}, u32[]{:S(2)}) collective-permute-start(bf16[256,512]{1,0:T(8,128)(2,1)S(1)} %fusion.27), channel_id=1, source_target_pairs={{0,2},{2,0},{1,3},{3,1},{4,6},{6,4},{5,7},{7,5},{8,10},{10,8},{9,1... | collective-permute-start | bytes 786440 | tf_op jit(solution)/shard_map/ppermute | solution.py:188
  18.1 16.2 %collective-permute-start = (bf16[256,512]{1,0:T(8,128)(2,1)S(1)}, bf16[256,512]{1,0:T(8,128)(2,1)S(1)}, u32[]{:S(2)}, u32[]{:S(2)}) collective-permute-start(bf16[256,512]{1,0:T(8,128)(2,1)S(1)} %convolution_convert_fusion.3), channel_id=1, source_target_pairs={{0,1},{1,0},{2,3},{3,2},{4,5},{5,4},{6,7},{7,6},{8,9},{9,8},{10,11... | collective-permute-start | bytes 786440 | tf_op jit(solution)/shard_map/ppermute | solution.py:190
  21.0 15.8 %collective-permute-start.5 = (bf16[256,512]{1,0:T(8,128)(2,1)S(1)}, bf16[256,512]{1,0:T(8,128)(2,1)S(1)}, u32[]{:S(2)}, u32[]{:S(2)}) collective-permute-start(bf16[256,512]{1,0:T(8,128)(2,1)S(1)} %fusion.27), channel_id=1, source_target_pairs={{0,8},{4,12},{8,0},{12,4},{1,9},{5,13},{9,1},{13,5},{2,10},{6,14},... | collective-permute-start | bytes 786440 | tf_op jit(solution)/shard_map/ppermute | solution.py:155
  25.8 15.0 %collective-permute-start.6 = (bf16[256,512]{1,0:T(8,128)(2,1)S(1)}, bf16[256,512]{1,0:T(8,128)(2,1)S(1)}, u32[]{:S(2)}, u32[]{:S(2)}) collective-permute-start(bf16[256,512]{1,0:T(8,128)(2,1)S(1)} %fusion.27), channel_id=1, source_target_pairs={{0,4},{4,8},{8,12},{12,0},{1,5},{5,9},{9,13},{13,1},{2,6},{6,10},{... | collective-permute-start | bytes 786440 | tf_op jit(solution)/shard_map/ppermute | solution.py:155
  28.1 12.7 %collective-permute-start.7 = (bf16[256,512]{1,0:T(8,128)(2,1)S(1)}, bf16[256,512]{1,0:T(8,128)(2,1)S(1)}, u32[]{:S(2)}, u32[]{:S(2)}) collective-permute-start(bf16[256,512]{1,0:T(8,128)(2,1)S(1)} %fusion.27), channel_id=1, source_target_pairs={{0,12},{4,0},{8,4},{12,8},{1,13},{5,1},{9,5},{13,9},{2,14},{6,2},{... | collective-permute-start | bytes 786440 | tf_op jit(solution)/shard_map/ppermute | solution.py:155
  32.3 16.0 %collective-permute-start.2 = (bf16[256,512]{1,0:T(8,128)(2,1)S(1)}, bf16[256,512]{1,0:T(8,128)(2,1)S(1)}, u32[]{:S(2)}, u32[]{:S(2)}) collective-permute-start(bf16[256,512]{1,0:T(8,128)(2,1)S(1)} %collective-permute-done.1), channel_id=1, source_target_pairs={{0,8},{4,12},{8,0},{12,4},{1,9},{5,13},{9,1},{13,5},{2,10},{6,14},... | collective-permute-start | bytes 786440 | tf_op jit(solution)/shard_map/ppermute | solution.py:155
  34.3 15.3 %collective-permute-start.3 = (bf16[256,512]{1,0:T(8,128)(2,1)S(1)}, bf16[256,512]{1,0:T(8,128)(2,1)S(1)}, u32[]{:S(2)}, u32[]{:S(2)}) collective-permute-start(bf16[256,512]{1,0:T(8,128)(2,1)S(1)} %collective-permute-done.1), channel_id=1, source_target_pairs={{0,4},{4,8},{8,12},{12,0},{1,5},{5,9},{9,13},{13,1},{2,6},{6,10},{... | collective-permute-start | bytes 786440 | tf_op jit(solution)/shard_map/ppermute | solution.py:155
  36.8 12.8 %collective-permute-start.4 = (bf16[256,512]{1,0:T(8,128)(2,1)S(1)}, bf16[256,512]{1,0:T(8,128)(2,1)S(1)}, u32[]{:S(2)}, u32[]{:S(2)}) collective-permute-start(bf16[256,512]{1,0:T(8,128)(2,1)S(1)} %collective-permute-done.1), channel_id=1, source_target_pairs={{0,12},{4,0},{8,4},{12,8},{1,13},{5,1},{9,5},{13,9},{2,14},{6,2},{... | collective-permute-start | bytes 786440 | tf_op jit(solution)/shard_map/ppermute | solution.py:155
  56.3 6.5 %collective-permute-start.8 = (f32[256,640]{1,0:T(8,128)S(1)}, f32[256,640]{1,0:T(8,128)S(1)}, u32[]{:S(2)}, u32[]{:S(2)}) collective-permute-start(f32[256,640]{1,0:T(8,128)S(1)} %shard_map.74), channel_id=1, source_target_pairs={{0,1},{1,0},{2,3},{3,2},{4,5},{5,4},{6,7},{7,6},{8,9},{9,8},{10,11... | collective-permute-start | bytes 1966088 | tf_op jit(solution)/shard_map/ppermute | solution.py:198
  69.9 0.7 copy-start.6
  69.9 21.0 %copy-start.1 = (bf16[512,1536]{1,0:T(8,128)(2,1)S(1)}, bf16[512,1536]{1,0:T(8,128)(2,1)}, u32[]{:S(2)}) copy-start(bf16[512,1536]{1,0:T(8,128)(2,1)} %param.14) | copy-start | bytes 4718596
  71.4 37.6 %all-to-all-start = ((bf16[32,8,1,512]{3,1,2,0:T(8,128)(2,1)}), bf16[32,8,1,512]{3,1,2,0:T(8,128)(2,1)S(1)}, u32[]{:S(2)}, u32[]{:S(2)}) async-start(bf16[32,8,1,512]{3,1,2,0:T(8,128)(2,1)} %fusion.36), calls=%async_computation | async-start | bytes 524288 | tf_op jit(solution)/shard_map/all_to_all | solution.py:205
  111.5 1.0 copy-start.4
  113.1 24.5 %copy-start.3 = (bf16[512,512]{1,0:T(8,128)(2,1)S(1)}, bf16[512,512]{1,0:T(8,128)(2,1)}, u32[]{:S(2)}) copy-start(bf16[512,512]{1,0:T(8,128)(2,1)} %param.15) | copy-start | bytes 1572868
